TPU v7x, 32 devices: a whole 2x2x4 slice. The times are simulated.
32 devices in a mesh: seq: 8 (over y, x, core), tp: 4 (over z).
Axes of the slice: x: 2, y: 2, z: 4, core: 2. Of those that a mesh axis runs over, the one named last changes fastest.
Arguments:
- projected: bfloat16 [1536, 3, 8192], P('seq', None, 'tp'), may hold values from -6 to 6
- feat_taps: float32 [7, 3, 8192], P(None, None, 'tp'), may hold values from -2.5 to 2.5
- filters: float32 [512, 128], P('tp'), may hold values from -1.5 to 1.5
- out_weight: bfloat16 [8192, 8192], P('tp'), may hold values from -0.09375 to 0.09375
- cotangent: bfloat16 [1536, 8192], P('seq', 'tp'), may hold values from -6 to 6
Outputs:
- output: bfloat16 [1536, 8192], P('seq', 'tp')
- input_grad: bfloat16 [1536, 3, 8192], P('seq', None, 'tp')
All inputs are finite; a program needn't handle non-finite values.
Results may differ from a plain program's by a relative error of at most 0.0095.
Values may be sent and summed in bfloat16 or wider, within the bound.
No kernel may reach another device: no remote copies, remote signals or barrier semaphores. Data moves between devices by JAX's collectives and lax.ppermute only.
A program may use at most 128 MiB of HBM per device.

v0:
```python
import jax
import jax.numpy as jnp
from jax import lax
from jax.sharding import PartitionSpec as P


def take_rows(source, start, count, time_axis):
    return lax.slice_in_dim(source, start, start + count, axis=time_axis)


def component(source, index):
    return source[index]


def causal_taps(extended, weights, out_rows, time_axis):
    tap_count = weights.shape[0]
    result = weights[0] * take_rows(extended, tap_count - 1, out_rows, time_axis)
    for delay in range(1, tap_count):
        result = result + weights[delay] * take_rows(
            extended, tap_count - 1 - delay, out_rows, time_axis
        )
    return result


def later_taps(extended, weights, out_rows, time_axis):
    result = weights[0] * take_rows(extended, 0, out_rows, time_axis)
    for delay in range(1, weights.shape[0]):
        result = result + weights[delay] * take_rows(extended, delay, out_rows, time_axis)
    return result


def forward_core(extended, feat_weights, kernel_taps, row_count):
    filt_len = kernel_taps.shape[0]
    stack_axis = extended.ndim - 1
    plain_axis = 1
    feats = causal_taps(extended, feat_weights, row_count + filt_len - 1, stack_axis)
    product = component(feats, 1) * component(feats, 2)
    conv = causal_taps(product, kernel_taps, row_count, plain_axis)
    tail_rows = take_rows(feats, filt_len - 1, row_count, stack_axis)
    query = component(tail_rows, 0)
    mixed = (query * conv).astype(jnp.bfloat16)
    return (mixed, query, conv, component(tail_rows, 1), component(tail_rows, 2))


def backward_core(
    signal_ext, query_ext, key_ext, value_ext, feat_weights, kernel_taps, row_count, mixed_rows
):
    feat_len = feat_weights.shape[0]
    plain_axis = 1
    conv_grad = later_taps(signal_ext, kernel_taps, mixed_rows, plain_axis)
    padding = [(0, 0), (0, 0)]
    padding[plain_axis] = (0, row_count + feat_len - 1 - mixed_rows)
    conv_grad = jnp.pad(conv_grad, padding)
    stacked = jnp.stack([query_ext, conv_grad * value_ext, conv_grad * key_ext], axis=0)
    stack_axis = 2
    return later_taps(stacked, feat_weights, row_count, stack_axis).astype(jnp.bfloat16)


def body(projected, feat_taps, filters, out_weight, cotangent):
    channels = projected.shape[2]
    feat_len = feat_taps.shape[0]
    filt_len = filters.shape[1]
    reach = filt_len + feat_len - 2
    group_size = channels // filters.shape[0]
    channel_kernel = jnp.repeat(filters, group_size, axis=0)
    shards = lax.axis_size("seq")
    slim = channels // shards
    position = lax.axis_index("seq")
    moved = jnp.transpose(projected, (1, 2, 0))
    regrouped = lax.all_to_all(moved, "seq", split_axis=1, concat_axis=2, tiled=True)
    seq_rows = regrouped.shape[2]
    local_kernel = lax.dynamic_slice_in_dim(channel_kernel, position * slim, slim, 0)
    kernel_taps = local_kernel.T[:, :, None]
    local_taps = lax.dynamic_slice_in_dim(feat_taps, position * slim, slim, 2)[..., None]
    extended = jnp.pad(regrouped, ((0, 0), (0, 0), (reach, 0)))
    mixed_part, query, conv, key_feat, value_feat = forward_core(
        extended, local_taps, kernel_taps, seq_rows
    )
    mixed = lax.all_to_all(mixed_part, "seq", split_axis=1, concat_axis=0, tiled=True)
    mixed_form = "cd,ct->dt"
    weight_cols = out_weight
    summed = lax.psum_scatter(
        jnp.einsum(mixed_form, weight_cols, mixed, preferred_element_type=jnp.float32).astype(
            jnp.bfloat16
        ),
        "tp",
        scatter_dimension=0,
        tiled=True,
    ).astype(jnp.float32)
    output = summed.T.astype(jnp.bfloat16)
    grad_form = "te,ce->ct"
    weight_cols = out_weight
    grad_mixed = jnp.einsum(
        grad_form,
        lax.all_gather(cotangent, "tp", axis=1, tiled=True),
        weight_cols,
        preferred_element_type=jnp.float32,
    )
    grad_part = lax.all_to_all(grad_mixed, "seq", split_axis=0, concat_axis=1, tiled=True)
    signal_grad = grad_part * query
    query_grad = grad_part * conv
    tail_pad = ((0, 0), (0, feat_len - 1))
    signal_ext = jnp.pad(signal_grad, ((0, 0), (0, filt_len - 1)))
    input_part = backward_core(
        signal_ext,
        jnp.pad(query_grad, tail_pad),
        jnp.pad(key_feat, tail_pad),
        jnp.pad(value_feat, tail_pad),
        local_taps,
        kernel_taps,
        seq_rows,
        seq_rows,
    )
    returned = lax.all_to_all(input_part, "seq", split_axis=2, concat_axis=1, tiled=True)
    input_grad = jnp.transpose(returned, (2, 0, 1))
    return (output, input_grad)


def solution(mesh):
    in_specs = (
        P("seq", None, "tp"),
        P(None, None, "tp"),
        P("tp", None),
        P("tp", None),
        P("seq", "tp"),
    )
    out_specs = (P("seq", "tp"), P("seq", None, "tp"))
    return jax.shard_map(body, mesh=mesh, in_specs=in_specs, out_specs=out_specs, check_vma=False)
```

profile of v0, /device:TPU:0, one launch (start us, length us, event | category | flops | bytes accessed | tf_op | source)
XLA Modules:
  0.0 311.3 jit_solution(12875204798442375766)
XLA Ops:
  7.2 0.7 all-gather.2.cloned.1.call-update
  7.9 6.9 %copy.14 = bf16[192,3,2048]{0,1,2:T(4,128)(2,1)} copy(bf16[192,3,2048]{2,0,1:T(8,128)(2,1)} %param.5) | data formatting | bytes 4718592 | tf_op args[0]
  14.9 5.2 %all-to-all-start = ((bf16[3,2048,192]{2,0,1:T(4,128)(2,1)}), bf16[3,2048,192]{2,0,1:T(4,128)(2,1)}, u32[]{:S(2)}, u32[]{:S(2)}) async-start(bf16[3,2048,192]{2,0,1:T(4,128)(2,1)} %bitcast.69), calls=%async_computation | async-start | bytes 8388608 | tf_op jit(solution)/shard_map/all_to_all | solution.py:70
  20.1 1.2 constant_dynamic-slice_fusion.5
  21.4 1.1 slice_reduce_fusion.121
  22.5 1.4 slice_reduce_fusion.127
  23.8 1.4 slice_reduce_fusion.122
  25.3 2.0 slice_reduce_fusion.126
  27.3 2.0 slice_reduce_fusion.125
  29.3 2.0 slice_reduce_fusion.124
  31.3 2.0 slice_reduce_fusion.123
  33.3 36.0 %all-to-all-done = bf16[3,2048,192]{2,0,1:T(4,128)(2,1)} async-done(((bf16[3,2048,192]{2,0,1:T(4,128)(2,1)}), bf16[3,2048,192]{2,0,1:T(4,128)(2,1)}, u32[]{:S(2)}, u32[]{:S(2)}) %all-to-all-start) | async-done | bytes 2359328 | tf_op jit(solution)/shard_map/all_to_all | solution.py:70
  69.3 6.9 %copy.23 = bf16[3,8,256,192]{2,3,1,0:T(8,128)(2,1)} copy(bf16[3,8,256,192]{3,0,2,1:T(4,128)(2,1)} %bitcast.1) | data formatting | bytes 4718592 | tf_op jit(solution)/shard_map/all_to_all | solution.py:70
  76.2 18.0 %fusion.143 = f32[2048,192]{0,1:T(8,128)S(1)} fusion(bf16[2048,8192]{1,0:T(8,128)(2,1)} %param.8, bf16[192,8192]{1,0:T(8,128)(2,1)} %all-gather.2.cloned.1.call-done), kind=kOutput, calls=%fused_computation.438 | convolution fusion | flops 6442450944 | bytes 38273024 | tf_op jit(solution)/shard_map/te,ce->ct/dot_general | solution.py:93
  94.2 1.3 copy.42
  95.5 3.6 %all-to-all-start.2 = ((f32[8,256,192]{1,2,0:T(8,128)}), f32[8,256,192]{1,2,0:T(8,128)S(1)}, u32[]{:S(2)}, u32[]{:S(2)}) async-start(f32[8,256,192]{1,2,0:T(8,128)} %bitcast.67), calls=%async_computation.3 | async-start | bytes 3145728 | tf_op jit(solution)/shard_map/all_to_all | solution.py:99
  99.1 10.0 %multiply_add_fusion = f32[3,256,1663]{1,2,0:T(8,128)S(1)} fusion(f32[3,256]{1,0:T(4,128)S(1)} %get-tuple-element.145, f32[3,256]{1,0:T(4,128)S(1)} %get-tuple-element.146, f32[3,256]{1,0:T(4,128)S(1)} %get-tuple-element.147, f32[3,256]{1,0:T(4,128)S(1)} %get-tuple-element.148, f32[3,256]{1,0:T(4,128)S(1)} %get-tuple-element.149, ...), kind=kLoop, calls=%fused_computation.2 | loop fusion | flops 25543680 | bytes 7489536 | tf_op jit(solution)/shard_map/add | solution.py:19
  109.1 2.2 copy-done.2
  111.6 8.4 %all-to-all-done.2 = f32[8,256,192]{1,2,0:T(8,128)S(1)} async-done(((f32[8,256,192]{1,2,0:T(8,128)}), f32[8,256,192]{1,2,0:T(8,128)S(1)}, u32[]{:S(2)}, u32[]{:S(2)}) %all-to-all-start.2) | async-done | bytes 1572896 | tf_op jit(solution)/shard_map/all_to_all | solution.py:99
  120.0 41.9 %bitcast_multiply_fusion.1 = (f32[256,1536]{0,1:T(8,128)}, f32[256,1536]{0,1:T(8,128)}) fusion(f32[8,256,192]{1,2,0:T(8,128)S(1)} %all-to-all-done.2, f32[256,1663]{0,1:T(8,128)S(1)} %fusion.8, f32[256]{0:T(256)S(1)} %get-tuple-element.3, f32[256]{0:T(256)S(1)} %get-tuple-element.4, f32[256]{0:T(256)S(1)} %get-tuple-element.5, f32[256]{0:T(256)S(1)} %get-tuple-element.6, ...), kind=kLoop, calls=%fused_computation.283 | loop fusion | flops 100663296 | bytes 206176256 | tf_op jit(solution)/shard_map/mul | solution.py:101
  161.9 3.2 %bitcast_multiply_fusion = (f32[256,1536]{0,1:T(8,128)S(1)}, bf16[256,1536]{0,1:T(8,128)(2,1)}) fusion(f32[8,256,192]{1,2,0:T(8,128)S(1)} %all-to-all-done.2, f32[3,256,1663]{1,2,0:T(8,128)} %copy-done.2, f32[256,1536]{0,1:T(8,128)} %get-tuple-element.131), kind=kLoop, calls=%fused_computation.282 | loop fusion | flops 1179648 | bytes 7077888 | tf_op jit(solution)/shard_map/mul | solution.py:100
  165.2 3.8 %all-to-all-start.1 = ((bf16[256,8,192]{0,2,1:T(8,128)(2,1)}), bf16[256,8,192]{0,2,1:T(8,128)(2,1)S(1)}, u32[]{:S(2)}, u32[]{:S(2)}) async-start(bf16[256,8,192]{0,2,1:T(8,128)(2,1)} %bitcast.72), calls=%async_computation.1 | async-start | bytes 1572864 | tf_op jit(solution)/shard_map/all_to_all | solution.py:79
  169.0 3.7 %slice_bitcast_fusion.1 = (f32[256,1536]{0,1:T(8,128)}, f32[256,1536]{0,1:T(8,128)}) fusion(f32[3,256,1663]{1,2,0:T(8,128)} %copy-done.2), kind=kLoop, calls=%fused_computation.25 | loop fusion | bytes 6291456 | tf_op jit(solution)/shard_map/squeeze | solution.py:12
  172.7 8.7 %all-to-all-done.1 = bf16[256,8,192]{0,2,1:T(8,128)(2,1)S(1)} async-done(((bf16[256,8,192]{0,2,1:T(8,128)(2,1)}), bf16[256,8,192]{0,2,1:T(8,128)(2,1)S(1)}, u32[]{:S(2)}, u32[]{:S(2)}) %all-to-all-start.1) | async-done | bytes 786464 | tf_op jit(solution)/shard_map/all_to_all | solution.py:79
  181.5 15.7 %fusion = bf16[8192,192]{0,1:T(8,128)(2,1)} fusion(bf16[2048,192]{0,1:T(8,128)(2,1)S(1)} %bitcast.77, bf16[2048,8192]{1,0:T(8,128)(2,1)} %param.8), kind=kOutput, calls=%fused_computation.1 | convolution fusion | flops 6444023808 | bytes 37486592 | tf_op jit(solution)/shard_map/cd,ct->dt/dot_general | solution.py:83
  198.2 43.8 %multiply_add_fusion.1 = f32[256,1536]{0,1:T(8,128)} fusion(f32[256,1536]{0,1:T(8,128)S(1)} %get-tuple-element.134, f32[256]{0:T(256)S(1)} %get-tuple-element.3, f32[256]{0:T(256)S(1)} %get-tuple-element.4, f32[256]{0:T(256)S(1)} %get-tuple-element.5, f32[256]{0:T(256)S(1)} %get-tuple-element.6, f32[256]{0:T(256)S(1)} %get-tuple-element.7, ...), kind=kLoop, calls=%fused_computation.284 | loop fusion | flops 100270080 | bytes 3276800 | tf_op jit(solution)/shard_map/add | solution.py:28
  242.1 1.3 copy-done.4
  243.9 1.7 multiply_bitcast_fusion.1
  246.0 4.0 %fusion.2 = bf16[3,256,1536]{1,2,0:T(8,128)(2,1)S(1)} fusion(f32[3,256,1542]{1,2,0:T(8,128)S(1)} %pad_maximum_fusion, f32[3,256]{1,0:T(4,128)S(1)} %get-tuple-element.145, f32[3,256]{1,0:T(4,128)S(1)} %get-tuple-element.146, f32[3,256]{1,0:T(4,128)S(1)} %get-tuple-element.147, f32[3,256]{1,0:T(4,128)S(1)} %get-tuple-element.148, ...), kind=kLoop, calls=%fused_computation.6 | loop fusion | flops 16515072 | bytes 35410944 | tf_op jit(solution)/shard_map/convert_element_type | solution.py:56
  250.0 12.0 %copy.19 = bf16[3,256,1536]{1,0,2:T(4,128)(2,1)S(1)} copy(bf16[3,256,1536]{1,2,0:T(8,128)(2,1)S(1)} %fusion.2) | data formatting | bytes 4718592 | tf_op jit(solution)/shard_map/convert_element_type | solution.py:56
  262.1 40.3 %all_to_all.74 = bf16[3,256,1536]{1,0,2:T(4,128)(2,1)S(1)} all-to-all(bf16[3,256,1536]{1,0,2:T(4,128)(2,1)S(1)} %copy.19), channel_id=1, replica_groups=mesh['seq'=8,'tp'=4] {'seq'}, dimensions={2} | all-to-all | bytes 4718592 | tf_op jit(solution)/shard_map/all_to_all | solution.py:114
  302.7 1.7 copy.33
  (90 shorter events, 2.4 us)
Async XLA Ops:
  7.2 14.1 %copy-start = (f32[128,128]{1,0:T(8,128)S(1)}, f32[128,128]{1,0:T(8,128)}, u32[]{:S(2)}) copy-start(f32[128,128]{1,0:T(8,128)} %param.7) | copy-start | bytes 196612
  7.2 69.0 %all-gather.2.cloned.1.call-start = ((), (), s32[]{:S(2)}) async-start(), calls=%async_computation.6 | async-start | bytes 3932160 | tf_op jit(solution)/shard_map/all_gather | solution.py:95
  14.9 54.4 %all-to-all-start = ((bf16[3,2048,192]{2,0,1:T(4,128)(2,1)}), bf16[3,2048,192]{2,0,1:T(4,128)(2,1)}, u32[]{:S(2)}, u32[]{:S(2)}) async-start(bf16[3,2048,192]{2,0,1:T(4,128)(2,1)} %bitcast.69), calls=%async_computation | async-start | bytes 8388608 | tf_op jit(solution)/shard_map/all_to_all | solution.py:70
  95.5 24.5 %all-to-all-start.2 = ((f32[8,256,192]{1,2,0:T(8,128)}), f32[8,256,192]{1,2,0:T(8,128)S(1)}, u32[]{:S(2)}, u32[]{:S(2)}) async-start(f32[8,256,192]{1,2,0:T(8,128)} %bitcast.67), calls=%async_computation.3 | async-start | bytes 3145728 | tf_op jit(solution)/shard_map/all_to_all | solution.py:99
  109.1 2.3 copy-start.2
  165.2 16.3 %all-to-all-start.1 = ((bf16[256,8,192]{0,2,1:T(8,128)(2,1)}), bf16[256,8,192]{0,2,1:T(8,128)(2,1)S(1)}, u32[]{:S(2)}, u32[]{:S(2)}) async-start(bf16[256,8,192]{0,2,1:T(8,128)(2,1)} %bitcast.72), calls=%async_computation.1 | async-start | bytes 1572864 | tf_op jit(solution)/shard_map/all_to_all | solution.py:79
  168.9 135.5 %reduce-scatter.2.cloned.1.call-start = ((), (), s32[]{:S(2)}) async-start(), calls=%async_computation.5 | async-start | bytes 3932160 | tf_op jit(solution)/shard_map/reduce_scatter | solution.py:82
  197.3 0.7 copy-start.6
  197.3 0.7 copy-start.7
  197.3 0.7 copy-start.8
  197.3 0.7 copy-start.9
  197.3 0.7 copy-start.10
  197.3 0.7 copy-start.11
  197.3 0.7 copy-start.12
  197.3 0.7 copy-start.13
  197.3 0.7 copy-start.14
  197.3 0.7 copy-start.15
  197.3 0.7 copy-start.16
  197.4 0.7 copy-start.17
  197.4 0.7 copy-start.18
  197.4 0.7 copy-start.19
  197.4 0.7 copy-start.20
  197.4 0.7 copy-start.23
  197.5 0.7 copy-start.33
  197.5 0.7 copy-start.34
  197.5 0.7 copy-start.35
  197.5 0.7 copy-start.36
  197.6 0.7 copy-start.37
  198.2 43.8 %copy-start.3 = (f32[256,1536]{0,1:T(8,128)S(1)}, f32[256,1536]{0,1:T(8,128)}, u32[]{:S(2)}) copy-start(f32[256,1536]{0,1:T(8,128)} %get-tuple-element.130) | copy-start | bytes 4718596
  242.0 1.4 copy-start.4
  242.0 1.9 copy-start.5
  302.7 1.7 copy-start.1
  (11 other events, 7.3 us)
Sparse Core Ops, SparseCore 0:
  9.6 66.1 all-gather.1
  197.7 60.5 reduce-scatter.1
where the time goes:
time: 312 us; the launch traced here: 311 us
  other arithmetic  105 us (34%)
  waiting for transfers between devices  53.9 us (17%)
  local copies, waits for them, and re-layouts  51 us (16%)
  blocking collectives  40.3 us (13%)
  matrix products  33.7 us (11%)
  between operations  14.6 us (5%)
  starting transfers between devices  12.6 us (4%)
    add x1, other arithmetic, later_taps(): result + weights[delay] * take_rows(extended, delay, out_rows, time_axis)  43.8 us
    mul x1, other arithmetic, body(): query_grad = grad_part * conv  41.9 us
    all_to_all x1, blocking collectives, body(): lax.all_to_all(input_part, 'seq', split_axis=2, concat_axis=1, tiled=True)  40.3 us
    all_to_all x1, waiting for transfers between devices, body(): lax.all_to_all(moved, 'seq', split_axis=1, concat_axis=2, tiled=True)  36 us
    dot_general x1, matrix products, body(): jnp.einsum(grad_form, lax.all_gather(cotangent, 'tp', axis=1, tiled=True)...  18 us
    dot_general x1, matrix products, body(): jnp.einsum(mixed_form, weight_cols, mixed, preferred_element_type=jnp.flo...  15.7 us
    convert_element_type x1, local copies, waits for them, and re-layouts, backward_core(): later_taps(stacked, feat_weights, row_count, stack_axis)  12 us
    unnamed x81, local copies, waits for them, and re-layouts  11.6 us
  transfers between devices with their start and end apart: 5, of which 3 were waited for; matrix products, arithmetic and copies ran while one was open for 34% of the time, Pallas kernels for 0%

commit v1 on v0

--- a/solution.py
+++ b/solution.py
@@ -2,6 +2,7 @@
 import jax.numpy as jnp
 from jax import lax
 from jax.sharding import PartitionSpec as P
+from jax.lax import all_to_all, axis_size
 
 
 def take_rows(source, start, count, time_axis):
@@ -76,7 +77,11 @@
     mixed_part, query, conv, key_feat, value_feat = forward_core(
         extended, local_taps, kernel_taps, seq_rows
     )
-    mixed = lax.all_to_all(mixed_part, "seq", split_axis=1, concat_axis=0, tiled=True)
+    row_out = axis_size("seq")
+    outcome_arr = jnp.split(mixed_part, row_out, 1)
+    kept_arr = jnp.stack(outcome_arr)
+    b_now = all_to_all(kept_arr, "seq", 0, 0)
+    mixed = jnp.concatenate(b_now, 0)
     mixed_form = "cd,ct->dt"
     weight_cols = out_weight
     summed = lax.psum_scatter(

time: 312 us -> 316 us (1.013)
  local copies, waits for them, and re-layouts: 51 us -> 56.2 us
    unnamed x81 -> x88, local copies, waits for them, and re-layouts: 11.6 us -> 16.1 us
  transfers between devices with their start and end apart: 5 -> 5, of which waited for: 3 -> 3; matrix products, arithmetic and copies ran while one was open for 34% -> 33% of each run, Pallas kernels for 0% -> 0%
where the time goes in v1:
time: 316 us
  other arithmetic  104 us (33%)
  local copies, waits for them, and re-layouts  56.2 us (18%)
  waiting for transfers between devices  53.9 us (17%)
  blocking collectives  40.3 us (13%)
  matrix products  34 us (11%)
  between operations  14.6 us (5%)
  starting transfers between devices  12.4 us (4%)
    add x1, other arithmetic, later_taps(): result + weights[delay] * take_rows(extended, delay, out_rows, time_axis)  43.8 us
    mul x1, other arithmetic, body(): query_grad = grad_part * conv  41.9 us
    all_to_all x1, blocking collectives, body(): lax.all_to_all(input_part, 'seq', split_axis=2, concat_axis=1, tiled=True)  40.3 us
    all_to_all x1, waiting for transfers between devices, body(): lax.all_to_all(moved, 'seq', split_axis=1, concat_axis=2, tiled=True)  36 us
    dot_general x1, matrix products, body(): jnp.einsum(grad_form, lax.all_gather(cotangent, 'tp', axis=1, tiled=True)...  18 us
    unnamed x88, local copies, waits for them, and re-layouts  16.1 us
    dot_general x1, matrix products, body(): jnp.einsum(mixed_form, weight_cols, mixed, preferred_element_type=jnp.flo...  16 us
    convert_element_type x1, local copies, waits for them, and re-layouts, backward_core(): later_taps(stacked, feat_weights, row_count, stack_axis)  12 us
  transfers between devices with their start and end apart: 5, of which 3 were waited for; matrix products, arithmetic and copies ran while one was open for 33% of the time, Pallas kernels for 0%

profile of v1, /device:TPU:0, one launch (start us, length us, event | category | flops | bytes accessed | tf_op | source)
XLA Modules:
  0.0 315.6 jit_solution(714221801025335574)
XLA Ops:
  7.2 0.7 all-gather.2.cloned.1.call-update
  7.9 6.9 %copy.13 = bf16[192,3,2048]{0,1,2:T(4,128)(2,1)} copy(bf16[192,3,2048]{2,0,1:T(8,128)(2,1)} %param.5) | data formatting | bytes 4718592 | tf_op args[0]
  14.9 5.2 %all-to-all-start = ((bf16[3,2048,192]{2,0,1:T(4,128)(2,1)}), bf16[3,2048,192]{2,0,1:T(4,128)(2,1)}, u32[]{:S(2)}, u32[]{:S(2)}) async-start(bf16[3,2048,192]{2,0,1:T(4,128)(2,1)} %bitcast.99), calls=%async_computation | async-start | bytes 8388608 | tf_op jit(solution)/shard_map/all_to_all | solution.py:71
  20.1 1.2 constant_dynamic-slice_fusion.5
  21.4 1.1 slice_reduce_fusion.121
  22.5 1.4 slice_reduce_fusion.127
  23.8 1.4 slice_reduce_fusion.122
  25.3 2.0 slice_reduce_fusion.126
  27.3 2.0 slice_reduce_fusion.125
  29.3 2.0 slice_reduce_fusion.124
  31.3 2.0 slice_reduce_fusion.123
  33.3 36.0 %all-to-all-done = bf16[3,2048,192]{2,0,1:T(4,128)(2,1)} async-done(((bf16[3,2048,192]{2,0,1:T(4,128)(2,1)}), bf16[3,2048,192]{2,0,1:T(4,128)(2,1)}, u32[]{:S(2)}, u32[]{:S(2)}) %all-to-all-start) | async-done | bytes 2359328 | tf_op jit(solution)/shard_map/all_to_all | solution.py:71
  69.3 6.9 %copy.22 = bf16[3,8,256,192]{2,3,1,0:T(8,128)(2,1)} copy(bf16[3,8,256,192]{3,0,2,1:T(4,128)(2,1)} %bitcast.1) | data formatting | bytes 4718592 | tf_op jit(solution)/shard_map/all_to_all | solution.py:71
  76.2 18.0 %fusion.151 = f32[2048,192]{0,1:T(8,128)S(1)} fusion(bf16[2048,8192]{1,0:T(8,128)(2,1)} %param.8, bf16[192,8192]{1,0:T(8,128)(2,1)} %all-gather.2.cloned.1.call-done), kind=kOutput, calls=%fused_computation.454 | convolution fusion | flops 6442450944 | bytes 38273024 | tf_op jit(solution)/shard_map/te,ce->ct/dot_general | solution.py:98
  94.2 1.3 copy.41
  95.5 3.6 %all-to-all-start.2 = ((f32[8,256,192]{1,2,0:T(8,128)}), f32[8,256,192]{1,2,0:T(8,128)S(1)}, u32[]{:S(2)}, u32[]{:S(2)}) async-start(f32[8,256,192]{1,2,0:T(8,128)} %bitcast.97), calls=%async_computation.3 | async-start | bytes 3145728 | tf_op jit(solution)/shard_map/all_to_all | solution.py:104
  99.1 10.0 %multiply_add_fusion = f32[3,256,1663]{1,2,0:T(8,128)S(1)} fusion(f32[3,256]{1,0:T(4,128)S(1)} %get-tuple-element.145, f32[3,256]{1,0:T(4,128)S(1)} %get-tuple-element.146, f32[3,256]{1,0:T(4,128)S(1)} %get-tuple-element.147, f32[3,256]{1,0:T(4,128)S(1)} %get-tuple-element.148, f32[3,256]{1,0:T(4,128)S(1)} %get-tuple-element.149, ...), kind=kLoop, calls=%fused_computation.2 | loop fusion | flops 25543680 | bytes 7489536 | tf_op jit(solution)/shard_map/add | solution.py:20
  109.1 2.2 copy-done.2
  111.6 8.4 %all-to-all-done.2 = f32[8,256,192]{1,2,0:T(8,128)S(1)} async-done(((f32[8,256,192]{1,2,0:T(8,128)}), f32[8,256,192]{1,2,0:T(8,128)S(1)}, u32[]{:S(2)}, u32[]{:S(2)}) %all-to-all-start.2) | async-done | bytes 1572896 | tf_op jit(solution)/shard_map/all_to_all | solution.py:104
  120.0 41.9 %bitcast_multiply_fusion.1 = (f32[256,1536]{0,1:T(8,128)}, f32[256,1536]{0,1:T(8,128)}) fusion(f32[8,256,192]{1,2,0:T(8,128)S(1)} %all-to-all-done.2, f32[256,1663]{0,1:T(8,128)S(1)} %fusion.8, f32[256]{0:T(256)S(1)} %get-tuple-element.3, f32[256]{0:T(256)S(1)} %get-tuple-element.4, f32[256]{0:T(256)S(1)} %get-tuple-element.5, f32[256]{0:T(256)S(1)} %get-tuple-element.6, ...), kind=kLoop, calls=%fused_computation.283 | loop fusion | flops 100663296 | bytes 206176256 | tf_op jit(solution)/shard_map/mul | solution.py:106
  161.9 2.3 bitcast_multiply_fusion
  169.5 3.5 %all-to-all-start.1 = ((bf16[8,256,192]{1,2,0:T(8,128)(2,1)}), bf16[8,256,192]{1,2,0:T(8,128)(2,1)S(1)}, u32[]{:S(2)}, u32[]{:S(2)}) async-start(bf16[8,256,192]{1,2,0:T(8,128)(2,1)} %fusion.142), calls=%async_computation.1 | async-start | bytes 1572864 | tf_op jit(solution)/shard_map/all_to_all | solution.py:83
  173.1 3.7 %slice_bitcast_fusion.1 = (f32[256,1536]{0,1:T(8,128)}, f32[256,1536]{0,1:T(8,128)}) fusion(f32[3,256,1663]{1,2,0:T(8,128)} %copy-done.2), kind=kLoop, calls=%fused_computation.25 | loop fusion | bytes 6291456 | tf_op jit(solution)/shard_map/squeeze | solution.py:13
  176.8 8.7 %all-to-all-done.1 = bf16[8,256,192]{1,2,0:T(8,128)(2,1)S(1)} async-done(((bf16[8,256,192]{1,2,0:T(8,128)(2,1)}), bf16[8,256,192]{1,2,0:T(8,128)(2,1)S(1)}, u32[]{:S(2)}, u32[]{:S(2)}) %all-to-all-start.1) | async-done | bytes 786464 | tf_op jit(solution)/shard_map/all_to_all | solution.py:83
  185.6 16.0 %fusion = bf16[8192,192]{0,1:T(8,128)(2,1)} fusion(bf16[2048,192]{0,1:T(8,128)(2,1)S(1)} %bitcast.106, bf16[2048,8192]{1,0:T(8,128)(2,1)} %param.8), kind=kOutput, calls=%fused_computation.1 | convolution fusion | flops 6444023808 | bytes 37486592 | tf_op jit(solution)/shard_map/cd,ct->dt/dot_general | solution.py:88
  202.5 43.8 %multiply_add_fusion.1 = f32[256,1536]{0,1:T(8,128)} fusion(f32[256,1536]{0,1:T(8,128)S(1)} %get-tuple-element.134, f32[256]{0:T(256)S(1)} %get-tuple-element.3, f32[256]{0:T(256)S(1)} %get-tuple-element.4, f32[256]{0:T(256)S(1)} %get-tuple-element.5, f32[256]{0:T(256)S(1)} %get-tuple-element.6, f32[256]{0:T(256)S(1)} %get-tuple-element.7, ...), kind=kLoop, calls=%fused_computation.284 | loop fusion | flops 100270080 | bytes 3276800 | tf_op jit(solution)/shard_map/add | solution.py:29
  246.5 1.3 copy-done.4
  248.2 1.7 multiply_bitcast_fusion.1
  250.3 4.0 %fusion.2 = bf16[3,256,1536]{1,2,0:T(8,128)(2,1)S(1)} fusion(f32[3,256,1542]{1,2,0:T(8,128)S(1)} %pad_maximum_fusion, f32[3,256]{1,0:T(4,128)S(1)} %get-tuple-element.145, f32[3,256]{1,0:T(4,128)S(1)} %get-tuple-element.146, f32[3,256]{1,0:T(4,128)S(1)} %get-tuple-element.147, f32[3,256]{1,0:T(4,128)S(1)} %get-tuple-element.148, ...), kind=kLoop, calls=%fused_computation.6 | loop fusion | flops 16515072 | bytes 35410944 | tf_op jit(solution)/shard_map/convert_element_type | solution.py:57
  254.3 12.0 %copy.18 = bf16[3,256,1536]{1,0,2:T(4,128)(2,1)S(1)} copy(bf16[3,256,1536]{1,2,0:T(8,128)(2,1)S(1)} %fusion.2) | data formatting | bytes 4718592 | tf_op jit(solution)/shard_map/convert_element_type | solution.py:57
  266.4 40.3 %all_to_all.60 = bf16[3,256,1536]{1,0,2:T(4,128)(2,1)S(1)} all-to-all(bf16[3,256,1536]{1,0,2:T(4,128)(2,1)S(1)} %copy.18), channel_id=1, replica_groups=mesh['seq'=8,'tp'=4] {'seq'}, dimensions={2} | all-to-all | bytes 4718592 | tf_op jit(solution)/shard_map/all_to_all | solution.py:119
  307.0 1.7 copy.32
  (98 shorter events, 7.6 us)
Async XLA Ops:
  7.2 14.1 %copy-start = (f32[128,128]{1,0:T(8,128)S(1)}, f32[128,128]{1,0:T(8,128)}, u32[]{:S(2)}) copy-start(f32[128,128]{1,0:T(8,128)} %param.7) | copy-start | bytes 196612
  7.2 69.0 %all-gather.2.cloned.1.call-start = ((), (), s32[]{:S(2)}) async-start(), calls=%async_computation.6 | async-start | bytes 3932160 | tf_op jit(solution)/shard_map/all_gather | solution.py:100
  14.9 54.4 %all-to-all-start = ((bf16[3,2048,192]{2,0,1:T(4,128)(2,1)}), bf16[3,2048,192]{2,0,1:T(4,128)(2,1)}, u32[]{:S(2)}, u32[]{:S(2)}) async-start(bf16[3,2048,192]{2,0,1:T(4,128)(2,1)} %bitcast.99), calls=%async_computation | async-start | bytes 8388608 | tf_op jit(solution)/shard_map/all_to_all | solution.py:71
  95.5 24.5 %all-to-all-start.2 = ((f32[8,256,192]{1,2,0:T(8,128)}), f32[8,256,192]{1,2,0:T(8,128)S(1)}, u32[]{:S(2)}, u32[]{:S(2)}) async-start(f32[8,256,192]{1,2,0:T(8,128)} %bitcast.97), calls=%async_computation.3 | async-start | bytes 3145728 | tf_op jit(solution)/shard_map/all_to_all | solution.py:104
  109.1 2.3 copy-start.2
  169.5 16.1 %all-to-all-start.1 = ((bf16[8,256,192]{1,2,0:T(8,128)(2,1)}), bf16[8,256,192]{1,2,0:T(8,128)(2,1)S(1)}, u32[]{:S(2)}, u32[]{:S(2)}) async-start(bf16[8,256,192]{1,2,0:T(8,128)(2,1)} %fusion.142), calls=%async_computation.1 | async-start | bytes 1572864 | tf_op jit(solution)/shard_map/all_to_all | solution.py:83
  173.0 135.7 %reduce-scatter.2.cloned.1.call-start = ((), (), s32[]{:S(2)}) async-start(), calls=%async_computation.5 | async-start | bytes 3932160 | tf_op jit(solution)/shard_map/reduce_scatter | solution.py:87
  201.6 0.7 copy-start.6
  201.6 0.7 copy-start.7
  201.6 0.7 copy-start.8
  201.6 0.7 copy-start.9
  201.6 0.7 copy-start.10
  201.6 0.7 copy-start.11
  201.6 0.7 copy-start.12
  201.6 0.7 copy-start.13
  201.6 0.7 copy-start.14
  201.6 0.7 copy-start.15
  201.6 0.7 copy-start.16
  201.7 0.7 copy-start.17
  201.7 0.7 copy-start.18
  201.7 0.7 copy-start.19
  201.7 0.7 copy-start.20
  201.7 0.7 copy-start.23
  201.8 0.7 copy-start.33
  201.8 0.7 copy-start.34
  201.8 0.7 copy-start.35
  201.8 0.7 copy-start.36
  201.9 0.7 copy-start.37
  202.5 43.8 %copy-start.3 = (f32[256,1536]{0,1:T(8,128)S(1)}, f32[256,1536]{0,1:T(8,128)}, u32[]{:S(2)}) copy-start(f32[256,1536]{0,1:T(8,128)} %get-tuple-element.130) | copy-start | bytes 4718596
  246.3 1.4 copy-start.4
  246.3 1.9 copy-start.5
  307.0 1.7 copy-start.1
  (11 other events, 7.3 us)
Sparse Core Ops, SparseCore 0:
  9.6 66.1 all-gather.1
  202.0 60.5 reduce-scatter.1
